TPU v7x, 32 devices: a whole 2x2x4 slice. The times are simulated.
32 devices in a mesh: grp: 2 (over y), wide: 4 (over z), col: 2 (over x), inc: 2 (over core).
Axes of the slice: x: 2, y: 2, z: 4, core: 2. Of those that a mesh axis runs over, the one named last changes fastest.
Arguments:
- values_in: bfloat16 [32, 64, 256, 512], P(('grp', 'col'), 'inc', 'wide'), parts along dimension 0, may hold values from -6 to 6
- shock_load: float32 [32], P(('grp', 'col')), parts along dimension 0, may hold values from -4 to 4
- price_field: float32 [128, 256, 512], P(('grp', 'inc'), 'wide'), parts along dimension 0, may hold values from -6 to 6
- rate_liquid: float32 [128, 256, 512], P(('grp', 'inc'), 'wide'), parts along dimension 0, may hold values from 0.05 to 0.5
- rate_illiquid: float32 [128, 256, 512], P(('grp', 'inc'), 'wide'), parts along dimension 0, may hold values from 0.05 to 0.5
- mask_liquid: int32 [128, 256, 512], P(('grp', 'inc'), 'wide'), parts along dimension 0, may hold values 0 or 1
- mask_illiquid: int32 [128, 256, 512], P(('grp', 'inc'), 'wide'), parts along dimension 0, may hold values 0 or 1
- jump_inverse: float32 [128, 64], P('grp'), parts along dimension 0, may hold values from -0.07 to 0.87
- coef_liquid: int32 [4096], replicated, may hold values from 0 to 127, as said below
- coef_illiquid: int32 [4096], replicated, may hold values from 0 to 255
- coef_income: int32 [4096], replicated, may hold values from 0 to 63
- owner: int32 [4096], replicated, may hold values from 0 to 7, as said below
Outputs:
- reduced: float32 [32, 8192], P(('grp', 'col'), ('wide', 'inc')), parts along dimension 0
There are 2 independent parts, one for each index of `grp`. A program takes and returns all parts, laid end to end along the dimension named above; an argument that names none is the same for every part. Nothing has to cross between parts.
Inputs may be any that keep to these rules, and one draw needn't show every extreme that they name: `coef_liquid`: every retained coefficient has liquid frequency below 128. No owner has more than 1024 rows, and some owner has exactly 1024.
All inputs are finite; a program needn't handle non-finite values. No bound on the sum of `mask_liquid` or of `mask_illiquid` on one device may be relied on, other than what follows from the above.
Results may differ from a plain program's by a relative error of at most 0.0003.
Values may be sent and summed in bfloat16 or wider, within the bound.
No kernel may reach another device: no remote copies, remote signals or barrier semaphores. Data moves between devices by JAX's collectives and lax.ppermute only.
A program may use at most 256 MiB of HBM per device.

v0:
```python
import jax
import jax.numpy as jnp
from jax import lax
from jax.sharding import PartitionSpec as P

NB = 512
NA = 256
NZ = 64
KBLOW = 128


def padded_2(cells, sides, width):
    for axis, dim in sides:
        count = lax.axis_size(axis)
        ends = count - 1
        head = lax.slice_in_dim(cells, 0, width, axis=dim)
        tail = lax.slice_in_dim(cells, cells.shape[dim] - width, cells.shape[dim], axis=dim)
        cells = jnp.concatenate(
            [
                lax.ppermute(tail, axis, [(i, (i + 1) % count) for i in range(ends)]),
                cells,
                lax.ppermute(head, axis, [((i + 1) % count, i) for i in range(ends)]),
            ],
            axis=dim,
        )
    return cells


def cosine_table(count):
    freq = jnp.arange(count, dtype=jnp.int32)[:, None]
    cell = jnp.arange(count, dtype=jnp.int32)[None, :]
    phase = (2 * cell + 1) * freq % (4 * count)
    angle = jnp.pi * phase.astype(jnp.float32) / (2.0 * count)
    first = jnp.where(freq == 0, jnp.sqrt(jnp.float32(0.5)), jnp.float32(1.0))
    return jnp.cos(angle) * jnp.sqrt(jnp.float32(2.0 / count)) * first


def slot_targets(owner, owners, capacity):
    onehot = (owner[:, None] == jnp.arange(owners, dtype=jnp.int32)[None, :]).astype(jnp.int32)
    before = jnp.cumsum(onehot, axis=0) - onehot
    slot = jnp.sum(before * onehot, axis=1)
    return owner * capacity + slot


def body(
    values_in,
    shock_load,
    price_field,
    rate_liquid,
    rate_illiquid,
    mask_liquid,
    mask_illiquid,
    jump_inverse,
    coef_liquid,
    coef_illiquid,
    coef_income,
    owner,
):
    high = lax.Precision.HIGHEST
    columns = values_in.shape[0]
    wide_pos = lax.axis_index("wide")
    wide_count = lax.axis_size("wide")
    padded = padded_2(values_in, (("wide", 2),), 1).astype(jnp.float32)
    center = padded[:, :, 1:-1]
    lower = jnp.where(wide_pos == 0, center[:, :, 0:1], padded[:, :, 0:1])
    upper = jnp.where(wide_pos == wide_count - 1, center[:, :, -1:], padded[:, :, -1:])
    fwd_a = jnp.concatenate([center[:, :, 1:], upper], axis=2) - center
    bwd_a = center - jnp.concatenate([lower, center[:, :, :-1]], axis=2)
    step_b = center[:, :, :, 1:] - center[:, :, :, :-1]
    zero_b = jnp.zeros(center.shape[:3] + (1,), jnp.float32)
    fwd_b = jnp.concatenate([step_b, zero_b], axis=3)
    bwd_b = jnp.concatenate([zero_b, step_b], axis=3)
    mask_b = mask_liquid.astype(jnp.float32)
    mask_a = mask_illiquid.astype(jnp.float32)
    load = shock_load[:, None, None, None]
    explicit = (
        center
        + rate_liquid * (mask_b * fwd_b - (1.0 - mask_b) * bwd_b)
        + rate_illiquid * (mask_a * fwd_a - (1.0 - mask_a) * bwd_a)
        + load * price_field
    )
    freq_rows = KBLOW
    table_b = cosine_table(NB)[:freq_rows]
    liquid_part = jnp.einsum("kb,czab->czak", table_b, explicit, precision=high)
    table_z = cosine_table(NZ)
    table_a = cosine_table(NA)
    owners = lax.axis_size(("wide", "inc"))
    capacity = 2 * owner.shape[0] // owners
    targets = slot_targets(owner, owners, capacity)
    blocks = lax.all_to_all(
        lax.all_to_all(liquid_part, "wide", split_axis=3, concat_axis=2, tiled=True),
        "inc",
        split_axis=3,
        concat_axis=1,
        tiled=True,
    )
    folded = jnp.dot(table_z, jump_inverse, precision=high)
    income_part = jnp.einsum("yz,czak->cyak", folded, blocks, precision=high)
    spectrum = jnp.einsum("ia,cjak->cjik", table_a, income_part, precision=high)
    local_rows = spectrum.shape[3]
    start = lax.axis_index(("wide", "inc")) * local_rows
    mine = (coef_liquid >= start) & (coef_liquid < start + local_rows)
    offset = jnp.clip(coef_liquid - start, 0, local_rows - 1)
    position = (coef_income * NA + coef_illiquid) * local_rows + offset
    flat = spectrum.reshape(columns, -1)
    kept = jnp.where(mine[None, :], jnp.take(flat, position, axis=1), jnp.float32(0.0))
    placed = jnp.zeros((columns, owners * capacity), jnp.float32).at[:, targets].set(kept)
    return lax.psum_scatter(placed, ("wide", "inc"), scatter_dimension=1, tiled=True)


def solution(mesh):
    placed = (
        P(("grp", "col"), "inc", "wide", None),
        P(("grp", "col")),
        P(("grp", "inc"), "wide", None),
        P(("grp", "inc"), "wide", None),
        P(("grp", "inc"), "wide", None),
        P(("grp", "inc"), "wide", None),
        P(("grp", "inc"), "wide", None),
        P("grp", None),
        P(),
        P(),
        P(),
        P(),
    )
    return jax.shard_map(
        body,
        mesh=mesh,
        in_specs=placed,
        out_specs=P(("grp", "col"), ("wide", "inc")),
        check_vma=False,
    )
```

profile of v0, /device:TPU:0, one launch (start us, length us, event | category | flops | bytes accessed | tf_op | source)
XLA Modules:
  0.0 726.5 jit_solution(2988138333981204830)
XLA Ops:
  6.5 0.0 copy-start
  6.5 3.4 fusion.115
  10.0 4.9 collective-permute-start
  15.0 1.3 collective-permute-start.1
  16.3 4.9 convert_element_type.28
  21.3 8.5 %broadcast_subtract_fusion = (f32[32,64,512]{2,1,0:T(8,128)}, f32[32,64,512]{2,1,0:T(8,128)}) fusion(s32[32,64,512]{2,1,0:T(8,128)} %param.18, s32[32,64,512]{2,1,0:T(8,128)} %param.17), kind=kLoop, calls=%fused_computation.43 | loop fusion | flops 4194304 | bytes 16777216 | tf_op jit(solution)/shard_map/sub | solution.py:79
  29.8 0.0 copy-done.2
  29.8 2.5 convert_element_type.29
  32.3 0.3 negate_select_fusion
  32.6 0.5 broadcast_compare_fusion.1
  33.1 0.0 collective-permute-done
  33.1 0.4 copy.22
  33.6 0.0 collective-permute-done.1
  33.6 0.4 copy.23
  34.0 21.0 %maximum_convert_fusion = f32[8,32,66,512]{3,2,1,0:T(8,128)} fusion(bf16[8,32,1,512]{3,2,1,0:T(2,128)(2,1)S(1)} %copy.23, bf16[8,32,64,512]{3,2,1,0:T(8,128)(2,1)} %param.12, bf16[8,32,1,512]{3,2,1,0:T(2,128)(2,1)S(1)} %copy.22), kind=kLoop, calls=%fused_computation.25 | loop fusion | flops 51904512 | bytes 51904512 | tf_op jit(solution)/shard_map/convert_element_type | solution.py:63
  55.0 0.0 copy-done.8
  55.0 47.7 %fusion.114 = (f32[8,32,63,512]{3,2,1,0:T(8,128)}, f32[8,32,63,512]{3,2,1,0:T(8,128)}) fusion(f32[8,32,66,512]{3,2,1,0:T(8,128)} %maximum_convert_fusion), kind=kLoop, calls=%fused_computation.141 | loop fusion | bytes 132120576 | tf_op jit(solution)/shard_map/slice | solution.py:68
  102.7 36.6 %slice_subtract_fusion = f32[8,32,64,511]{3,2,1,0:T(8,128)} fusion(f32[8,32,66,512]{3,2,1,0:T(8,128)} %maximum_convert_fusion), kind=kLoop, calls=%fused_computation.2 | loop fusion | flops 8372224 | bytes 100466688 | tf_op jit(solution)/shard_map/sub | solution.py:69
  139.4 0.0 slice-start
  139.4 4.9 broadcast_select_fusion
  144.2 0.0 copy-done.1
  144.3 0.0 copy-done.5
  144.3 74.5 %fusion.5 = f32[8,32,64,128]{3,2,1,0:T(8,128)} fusion(f32[8,32,1,512]{3,2,1,0:T(1,128)S(1)} %get-tuple-element.10, f32[8,32,63,512]{3,2,1,0:T(8,128)} %get-tuple-element.8, f32[8,32,63,512]{3,2,1,0:T(8,128)} %get-tuple-element.7, f32[8,32,1,512]{3,2,1,0:T(1,128)S(1)} %get-tuple-element.9, f32[8,32,66,512]{3,2,1,0:T(8,128)} %maximum_convert_fusion, ...), kind=kOutput, calls=%fused_computation.9 | convolution fusion | flops 13019512832 | bytes 173409280 | tf_op jit(solution)/shard_map/kb,czab->czak/dot_general | solution.py:84
  218.8 16.7 %copy.24 = f32[8,32,64,128]{2,1,0,3:T(8,128)} copy(f32[8,32,64,128]{3,2,1,0:T(8,128)} %fusion.5) | data formatting | bytes 16777216 | tf_op jit(solution)/shard_map/kb,czab->czak/dot_general | solution.py:84
  235.5 14.4 %reshape.110 = f32[4,1,524288]{2,1,0:T(1,128)} reshape(f32[128,8,32,64]{3,2,1,0:T(8,128)} %bitcast.55) | data formatting | bytes 16777216
  249.9 5.9 all-to-all-start
  255.9 2.3 reduce-window.6
  258.2 0.3 slice_reduce_fusion
  258.5 0.2 reduce-window.9
  258.7 0.0 copy-done
  258.7 0.3 convolution_bitcast_fusion
  259.0 0.1 add_bitcast_fusion
  259.1 0.1 fusion.71
  259.3 180.0 %all-to-all-done = f32[4,1,524288]{2,1,0:T(1,128)} async-done(((f32[4,1,524288]{2,1,0:T(1,128)}), f32[4,1,524288]{2,1,0:T(1,128)}, u32[]{:S(2)}, u32[]{:S(2)}) %all-to-all-start) | async-done | bytes 8388640 | tf_op jit(solution)/shard_map/all_to_all | solution.py:91
  439.4 0.5 broadcast.191
  439.9 28.4 %reduce.2 = f32[4,524288]{1,0:T(4,128)} reduce(f32[4,1,524288]{2,1,0:T(1,128)} %all-to-all-done, f32[]{:T(128)} %broadcast.191), dimensions={1}, to_apply=%all_to_all.26.reduce_sub_computation | reduce | bytes 16777220 | tf_op jit(solution)/shard_map/all_to_all | solution.py:91
  468.3 16.8 %reshape.111 = f32[128,8,32,64]{3,2,1,0:T(8,128)} reshape(f32[4,524288]{1,0:T(4,128)} %reduce.2) | data formatting | bytes 16777216
  485.0 21.0 %copy.39 = f32[8,32,4,64,32]{3,2,1,0,4:T(4,128)} copy(f32[8,32,4,64,32]{3,1,0,4,2:T(8,128)} %bitcast.56) | data formatting | bytes 16777216 | tf_op jit(solution)/shard_map/all_to_all | solution.py:91
  506.0 15.9 %reshape.98 = f32[8,32,256,32]{2,1,0,3:T(8,128)} reshape(f32[8,32,4,64,32]{3,2,1,0,4:T(4,128)} %copy.39) | data formatting | bytes 16777216 | tf_op jit(solution)/shard_map/all_to_all | solution.py:91
  521.9 12.1 %all_to_all.36 = f32[8,32,256,32]{2,1,0,3:T(8,128)S(1)} all-to-all(f32[8,32,256,32]{2,1,0,3:T(8,128)} %reshape.98), channel_id=1, replica_groups=mesh['grp'=2,'wide'=4,'col'=2,'inc'=2] {'inc'}, dimensions={3} | all-to-all | bytes 16777216 | tf_op jit(solution)/shard_map/all_to_all | solution.py:90
  534.0 6.7 copy.29
  540.6 13.7 %fusion.37 = f32[8,64,256,16]{2,1,3,0:T(8,128)S(1)} fusion(f32[64,64,1,1]{1,0,3,2:T(8,128)S(1)} %convolution_bitcast_fusion, f32[8,64,256,16]{2,3,1,0:T(8,128)S(1)} %bitcast.57), kind=kOutput, calls=%fused_computation.39 | convolution fusion | flops 1610612736 | bytes 16793600 | tf_op jit(solution)/shard_map/yz,czak->cyak/dot_general | solution.py:98
  554.4 13.7 %fusion.34 = f32[8,64,256,16]{2,3,1,0:T(8,128)} fusion(f32[8,64,256,16]{2,1,3,0:T(8,128)S(1)} %fusion.37, f32[256]{0:T(256)S(1)} %fusion.99, s32[256]{0:T(256)S(1)} %multiply_add_fusion.1), kind=kOutput, calls=%fused_computation.38 | convolution fusion | flops 6443433984 | bytes 16779264 | tf_op jit(solution)/shard_map/ia,cjak->cjik/dot_general | solution.py:99
  568.1 61.8 %copy.41 = f32[8,64,256,16]{0,3,2,1:T(8,128)} copy(f32[8,64,256,16]{2,3,1,0:T(8,128)} %fusion.34) | data formatting | bytes 16777216 | tf_op jit(solution)/shard_map/reshape | solution.py:105
  629.9 38.5 %scatter_custom_fusion = f32[8,8192]{0,1:T(8,128)} fusion(s32[4096]{0:T(1024)S(1)} %get-tuple-element.17, f32[]{:T(128)} %constant.42.clone.1, f32[]{:T(128)} %constant.125.clone.1, pred[4096]{0:T(1024)(128)(4,1)S(1)} %compare_and_fusion.1, pred[4096]{0:T(1024)(128)(4,1)S(1)} %compare_and_fusion, f32[8,262144]{0,1:T(8,128)} %bitcast.17, ...), kind=kCustom, calls=%fused_computation.40 | custom fusion | flops 65536 | bytes 134505984 | tf_op jit(solution)/shard_map/scatter | solution.py:107
  668.4 0.0 reduce-scatter.2.cloned.1.call-update
  668.5 49.2 %reduce-scatter.2.cloned.1.call-done = f32[8,1024]{0,1:T(8,128)} async-done(((f32[8,8192]{0,1:T(8,128)}), f32[8,1024]{0,1:T(8,128)}) %reduce-scatter.2.cloned.1.call-update) | async-done | bytes 32784 | tf_op jit(solution)/shard_map/reduce_scatter | solution.py:108
  717.6 1.8 copy.34
  (26 shorter events, 0.2 us)
Async XLA Ops:
  6.5 252.2 %copy-start = (f32[64,64]{1,0:T(8,128)S(1)}, f32[64,64]{1,0:T(8,128)}, u32[]{:S(2)}) copy-start(f32[64,64]{1,0:T(8,128)} %param.19) | copy-start | bytes 49156
  6.5 23.2 %copy-start.2 = (s32[32,64,512]{2,1,0:T(8,128)S(1)}, s32[32,64,512]{2,1,0:T(8,128)}, u32[]{:S(2)}) copy-start(s32[32,64,512]{2,1,0:T(8,128)} %param.18) | copy-start | bytes 12582916
  10.0 23.1 %collective-permute-start = (bf16[8,32,1,512]{3,1,2,0:T(8,128)(2,1)S(1)}, bf16[8,32,1,512]{3,1,2,0:T(8,128)(2,1)S(1)}, u32[]{:S(2)}, u32[]{:S(2)}) collective-permute-start(bf16[8,32,1,512]{3,1,2,0:T(8,128)(2,1)S(1)} %copy.44), channel_id=1, source_target_pairs={{0,4},{4,8},{8,12},{1,5},{5,9},{9,13},{2,6},{6,10},{10,14},{3,7},{... | collective-permute-start | bytes 786440 | tf_op jit(solution)/shard_map/ppermute | solution.py:20
  15.0 18.6 %collective-permute-start.1 = (bf16[8,32,1,512]{3,1,2,0:T(8,128)(2,1)S(1)}, bf16[8,32,1,512]{3,1,2,0:T(8,128)(2,1)S(1)}, u32[]{:S(2)}, u32[]{:S(2)}) collective-permute-start(bf16[8,32,1,512]{3,1,2,0:T(8,128)(2,1)S(1)} %copy.45), channel_id=1, source_target_pairs={{4,0},{8,4},{12,8},{5,1},{9,5},{13,9},{6,2},{10,6},{14,10},{7,3},{... | collective-permute-start | bytes 786440 | tf_op jit(solution)/shard_map/ppermute | solution.py:22
  32.3 22.7 %copy-start.8 = (f32[512]{0:T(512)}, f32[512]{0:T(512)S(1)}, u32[]{:S(2)}) copy-start(f32[512]{0:T(512)S(1)} %select_multiply_fusion) | copy-start | bytes 6148
  139.4 4.9 copy-start.1
  139.4 4.9 copy-start.5
  139.4 4.9 slice-start
  235.5 20.3 %copy-start.3 = (s32[4096]{0:T(1024)S(1)}, s32[4096]{0:T(1024)}, u32[]{:S(2)}) copy-start(s32[4096]{0:T(1024)} %param.23) | copy-start | bytes 49156
  235.5 23.7 %copy-start.4 = (s32[4096]{0:T(1024)S(1)}, s32[4096]{0:T(1024)}, u32[]{:S(2)}) copy-start(s32[4096]{0:T(1024)} %param.20) | copy-start | bytes 49156
  235.5 23.8 %copy-start.6 = (s32[4096]{0:T(1024)S(1)}, s32[4096]{0:T(1024)}, u32[]{:S(2)}) copy-start(s32[4096]{0:T(1024)} %param.21) | copy-start | bytes 49156
  235.5 23.8 %copy-start.7 = (s32[4096]{0:T(1024)S(1)}, s32[4096]{0:T(1024)}, u32[]{:S(2)}) copy-start(s32[4096]{0:T(1024)} %param.22) | copy-start | bytes 49156
  249.9 189.4 %all-to-all-start = ((f32[4,1,524288]{2,1,0:T(1,128)}), f32[4,1,524288]{2,1,0:T(1,128)}, u32[]{:S(2)}, u32[]{:S(2)}) async-start(f32[4,1,524288]{2,1,0:T(1,128)} %reshape.110), calls=%async_computation | async-start | bytes 16777216 | tf_op jit(solution)/shard_map/all_to_all | solution.py:91
  255.9 461.8 %reduce-scatter.2.cloned.1.call-start = ((), (), s32[]{:S(2)}) async-start(), calls=%async_computation.3 | async-start | bytes 4718592 | tf_op jit(solution)/shard_map/reduce_scatter | solution.py:108
Sparse Core Ops, SparseCore 0:
  668.6 49.0 reduce-scatter.1
where the time goes:
time: 733 us; the launch traced here: 727 us
  waiting for transfers between devices  229 us (31%)
  local copies, waits for them, and re-layouts  208 us (28%)
  other arithmetic  149 us (20%)
  matrix products  102 us (14%)
  between operations  13.8 us (2%)
  starting transfers between devices  12.2 us (2%)
  blocking collectives  12.1 us (2%)
    all_to_all x1, waiting for transfers between devices, body(): lax.all_to_all(liquid_part, 'wide', split_axis=3, concat_axis=2, tiled=True)  180 us
    dot_general x1, matrix products, body(): liquid_part = jnp.einsum('kb,czab->czak', table_b, explicit, precision=high)  74.5 us
    reshape x1, local copies, waits for them, and re-layouts, body(): flat = spectrum.reshape(columns, -1)  61.8 us
    reduce_scatter x1, waiting for transfers between devices, body(): lax.psum_scatter(placed, ('wide', 'inc'), scatter_dimension=1, tiled=True)  49.2 us
    slice x1, local copies, waits for them, and re-layouts, body(): bwd_a = center - jnp.concatenate([lower, center[:, :, :-1]], axis=2)  47.7 us
    scatter x1, other arithmetic, body(): jnp.zeros((columns, owners * capacity), jnp.float32).at[:, targets]  38.5 us
    all_to_all x3, local copies, waits for them, and re-layouts, body(): lax.all_to_all(liquid_part, 'wide', split_axis=3, concat_axis=2, tiled=True)  37.4 us
    sub x1, other arithmetic, body(): step_b = center[:, :, :, 1:] - center[:, :, :, :-1]  36.6 us
  transfers between devices with their start and end apart: 4, of which 2 were waited for; matrix products, arithmetic and copies ran while one was open for 3% of the time, Pallas kernels for 0%

commit v1 on v0

--- a/solution.py
+++ b/solution.py
@@ -7,6 +7,15 @@
 NA = 256
 NZ = 64
 KBLOW = 128
+derive_masks_by_axis = lambda view, along_axis: jnp.concatenate(
+    lax.all_to_all(
+        jnp.stack(jnp.split(view, lax.axis_size(along_axis), 3), axis=0),
+        along_axis,
+        split_axis=0,
+        concat_axis=0,
+    ),
+    2,
+)
 
 
 def padded_2(cells, sides, width):
@@ -88,11 +97,7 @@
     capacity = 2 * owner.shape[0] // owners
     targets = slot_targets(owner, owners, capacity)
     blocks = lax.all_to_all(
-        lax.all_to_all(liquid_part, "wide", split_axis=3, concat_axis=2, tiled=True),
-        "inc",
-        split_axis=3,
-        concat_axis=1,
-        tiled=True,
+        derive_masks_by_axis(liquid_part, "wide"), "inc", split_axis=3, concat_axis=1, tiled=True
     )
     folded = jnp.dot(table_z, jump_inverse, precision=high)
     income_part = jnp.einsum("yz,czak->cyak", folded, blocks, precision=high)

time: 733 us -> 790 us (1.078)
  local copies, waits for them, and re-layouts: 208 us -> 244 us
  other arithmetic: 149 us -> 170 us
    another operation x0 -> x2, local copies, waits for them, and re-layouts: none -> 47.9 us  [jnp.stack(jnp.split(view, lax.axis_size(along_axis), 3), axis=0)]
    reshape x0 -> x3, local copies, waits for them, and re-layouts: none -> 42.1 us  [jnp.concatenate(lax.all_to_all(jnp.stack(jnp.split(view, lax.axis_size(al...]
    all_to_all x4 -> x2, local copies, waits for them, and re-layouts: 44 us -> 7.16 us  [the longest x1 6.65 us: body(): lax.all_to_all(derive_masks_by_axis(liquid_part, 'wide'), 'inc', split_ax...]
    another operation x2 -> x3, other arithmetic: 2.5 us -> 23.6 us  [the longest x1 21.1 us: jnp.stack(jnp.split(view, lax.axis_size(along_axis), 3), axis=0)]
    dot_general x1 -> x0, local copies, waits for them, and re-layouts: 16.7 us -> none  [body(): liquid_part = jnp.einsum('kb,czab->czak', table_b, explicit, precision=high)]
where the time goes in v1:
time: 790 us; the launch traced here: 784 us
  local copies, waits for them, and re-layouts  244 us (31%)
  waiting for transfers between devices  229 us (29%)
  other arithmetic  170 us (22%)
  matrix products  102 us (13%)
  between operations  13.9 us (2%)
  starting transfers between devices  12.2 us (2%)
  blocking collectives  12.1 us (2%)
    all_to_all x1, waiting for transfers between devices, lax.all_to_all(jnp.stack(jnp.split(view, lax.axis_size(along_axis), 3), a...  180 us
    dot_general x1, matrix products, body(): liquid_part = jnp.einsum('kb,czab->czak', table_b, explicit, precision=high)  74.4 us
    reshape x1, local copies, waits for them, and re-layouts, body(): flat = spectrum.reshape(columns, -1)  61.7 us
    reduce_scatter x1, waiting for transfers between devices, body(): lax.psum_scatter(placed, ('wide', 'inc'), scatter_dimension=1, tiled=True)  49.1 us
    another operation x2, local copies, waits for them, and re-layouts, jnp.stack(jnp.split(view, lax.axis_size(along_axis), 3), axis=0)  47.9 us
    slice x1, local copies, waits for them, and re-layouts, body(): bwd_a = center - jnp.concatenate([lower, center[:, :, :-1]], axis=2)  47.7 us
    reshape x3, local copies, waits for them, and re-layouts, jnp.concatenate(lax.all_to_all(jnp.stack(jnp.split(view, lax.axis_size(al...  42.1 us
    scatter x1, other arithmetic, body(): jnp.zeros((columns, owners * capacity), jnp.float32).at[:, targets]  38.6 us
  transfers between devices with their start and end apart: 4, of which 2 were waited for; matrix products, arithmetic and copies ran while one was open for 3% of the time, Pallas kernels for 0%

profile of v1, /device:TPU:0, one launch (start us, length us, event | category | flops | bytes accessed | tf_op | source)
XLA Modules:
  0.0 783.6 jit_solution(13779511846307264830)
XLA Ops:
  6.5 0.0 copy-start
  6.5 3.4 fusion.115
  10.0 4.9 collective-permute-start
  15.0 1.3 collective-permute-start.1
  16.3 4.9 convert_element_type.28
  21.3 8.5 %broadcast_subtract_fusion = (f32[32,64,512]{2,1,0:T(8,128)}, f32[32,64,512]{2,1,0:T(8,128)}) fusion(s32[32,64,512]{2,1,0:T(8,128)} %param.18, s32[32,64,512]{2,1,0:T(8,128)} %param.17), kind=kLoop, calls=%fused_computation.48 | loop fusion | flops 4194304 | bytes 16777216 | tf_op jit(solution)/shard_map/sub | solution.py:88
  29.8 0.0 copy-done.2
  29.8 2.5 convert_element_type.29
  32.3 0.3 negate_select_fusion
  32.5 0.5 broadcast_compare_fusion.1
  33.1 0.0 collective-permute-done
  33.1 0.4 copy.21
  33.5 0.0 collective-permute-done.1
  33.5 0.4 copy.22
  34.0 21.2 %maximum_convert_fusion = f32[8,32,66,512]{3,2,1,0:T(8,128)} fusion(bf16[8,32,1,512]{3,2,1,0:T(2,128)(2,1)S(1)} %copy.22, bf16[8,32,64,512]{3,2,1,0:T(8,128)(2,1)} %param.12, bf16[8,32,1,512]{3,2,1,0:T(2,128)(2,1)S(1)} %copy.21), kind=kLoop, calls=%fused_computation.26 | loop fusion | flops 51904512 | bytes 51904512 | tf_op jit(solution)/shard_map/convert_element_type | solution.py:72
  55.2 0.0 copy-done.8
  55.2 47.7 %fusion.114 = (f32[8,32,63,512]{3,2,1,0:T(8,128)}, f32[8,32,63,512]{3,2,1,0:T(8,128)}) fusion(f32[8,32,66,512]{3,2,1,0:T(8,128)} %maximum_convert_fusion), kind=kLoop, calls=%fused_computation.146 | loop fusion | bytes 132120576 | tf_op jit(solution)/shard_map/slice | solution.py:77
  102.9 36.5 %slice_subtract_fusion = f32[8,32,64,511]{3,2,1,0:T(8,128)} fusion(f32[8,32,66,512]{3,2,1,0:T(8,128)} %maximum_convert_fusion), kind=kLoop, calls=%fused_computation.2 | loop fusion | flops 8372224 | bytes 100466688 | tf_op jit(solution)/shard_map/sub | solution.py:78
  139.4 0.0 slice-start
  139.4 4.9 broadcast_select_fusion
  144.3 74.4 %fusion.5 = f32[8,32,64,128]{3,2,1,0:T(8,128)} fusion(f32[8,32,1,512]{3,2,1,0:T(1,128)S(1)} %get-tuple-element.10, f32[8,32,63,512]{3,2,1,0:T(8,128)} %get-tuple-element.8, f32[8,32,63,512]{3,2,1,0:T(8,128)} %get-tuple-element.7, f32[8,32,1,512]{3,2,1,0:T(1,128)S(1)} %get-tuple-element.9, f32[8,32,66,512]{3,2,1,0:T(8,128)} %maximum_convert_fusion, ...), kind=kOutput, calls=%fused_computation.9 | convolution fusion | flops 13019512832 | bytes 173409280 | tf_op jit(solution)/shard_map/kb,czab->czak/dot_general | solution.py:93
  218.7 23.3 %slice_bitcast_fusion.3 = (f32[1,8,32,64,32]{4,3,2,1,0:T(8,128)S(1)}, f32[1,8,32,64,32]{4,3,2,1,0:T(8,128)}, f32[1,8,32,64,32]{4,3,2,1,0:T(8,128)}, f32[1,8,32,64,32]{4,3,2,1,0:T(8,128)}) fusion(f32[8,32,64,128]{3,2,1,0:T(8,128)} %fusion.5), kind=kLoop, calls=%fused_computation.38 | loop fusion | bytes 16777216 | tf_op jit(solution)/shard_map/stack | solution.py:12
  242.1 21.1 %pad_maximum_fusion = f32[4,8,32,64,32]{4,3,2,1,0:T(8,128)} fusion(f32[1,8,32,64,32]{4,3,2,1,0:T(8,128)} %get-tuple-element.14, f32[1,8,32,64,32]{4,3,2,1,0:T(8,128)} %get-tuple-element.15, f32[1,8,32,64,32]{4,3,2,1,0:T(8,128)} %get-tuple-element.16, f32[1,8,32,64,32]{4,3,2,1,0:T(8,128)S(1)} %get-tuple-element.13), kind=kLoop, calls=%fused_computation.16 | loop fusion | flops 6291456 | bytes 16777216 | tf_op jit(solution)/shard_map/stack | solution.py:12
  263.1 24.6 %copy.23 = f32[4,8,32,64,32]{3,4,2,1,0:T(8,128)} copy(f32[4,8,32,64,32]{4,3,2,1,0:T(8,128)} %pad_maximum_fusion) | data formatting | bytes 16777216 | tf_op jit(solution)/shard_map/stack | solution.py:12
  287.7 14.4 %reshape.118 = f32[4,1,524288]{2,1,0:T(1,128)} reshape(f32[4,8,32,32,64]{4,3,2,1,0:T(8,128)} %bitcast.63) | data formatting | bytes 16777216
  302.1 5.9 all-to-all-start
  308.0 2.3 reduce-window.6
  310.3 0.3 slice_reduce_fusion
  310.6 0.2 reduce-window.9
  310.9 0.3 convolution_bitcast_fusion
  311.2 0.1 add_bitcast_fusion
  311.3 0.1 fusion.71
  311.5 180.0 %all-to-all-done = f32[4,1,524288]{2,1,0:T(1,128)} async-done(((f32[4,1,524288]{2,1,0:T(1,128)}), f32[4,1,524288]{2,1,0:T(1,128)}, u32[]{:S(2)}, u32[]{:S(2)}) %all-to-all-start) | async-done | bytes 8388640 | tf_op jit(solution)/shard_map/all_to_all | solution.py:11
  491.5 0.5 broadcast.191
  492.0 28.4 %reduce.2 = f32[4,524288]{1,0:T(4,128)} reduce(f32[4,1,524288]{2,1,0:T(1,128)} %all-to-all-done, f32[]{:T(128)} %broadcast.191), dimensions={1}, to_apply=%all_to_all.16.reduce_sub_computation | reduce | bytes 16777220 | tf_op jit(solution)/shard_map/all_to_all | solution.py:11
  520.5 16.8 %reshape.119 = f32[4,8,32,32,64]{4,3,2,1,0:T(8,128)} reshape(f32[4,524288]{1,0:T(4,128)} %reduce.2) | data formatting | bytes 16777216
  537.2 7.4 bitcast_bitcast_fusion.1
  544.6 18.7 %copy.36 = f32[8,32,4,64,32]{3,2,1,0,4:T(4,128)} copy(f32[8,32,4,64,32]{3,4,1,0,2:T(8,128)S(1)} %bitcast_bitcast_fusion.1) | data formatting | bytes 16777216 | tf_op jit(solution)/shard_map/reshape | solution.py:10
  563.4 15.9 %reshape.106 = f32[8,32,256,32]{2,1,0,3:T(8,128)} reshape(f32[8,32,4,64,32]{3,2,1,0,4:T(4,128)} %copy.36) | data formatting | bytes 16777216 | tf_op jit(solution)/shard_map/reshape | solution.py:10
  579.3 12.1 %all_to_all.23 = f32[8,32,256,32]{2,1,0,3:T(8,128)S(1)} all-to-all(f32[8,32,256,32]{2,1,0,3:T(8,128)} %reshape.106), channel_id=1, replica_groups=mesh['grp'=2,'wide'=4,'col'=2,'inc'=2] {'inc'}, dimensions={3} | all-to-all | bytes 16777216 | tf_op jit(solution)/shard_map/all_to_all | solution.py:99
  591.4 6.7 copy.27
  598.0 13.5 %fusion.37 = f32[8,64,256,16]{2,1,3,0:T(8,128)S(1)} fusion(f32[64,64,1,1]{1,0,3,2:T(8,128)S(1)} %convolution_bitcast_fusion, f32[8,64,256,16]{2,3,1,0:T(8,128)S(1)} %bitcast.64), kind=kOutput, calls=%fused_computation.44 | convolution fusion | flops 1610612736 | bytes 16793600 | tf_op jit(solution)/shard_map/yz,czak->cyak/dot_general | solution.py:103
  611.5 13.8 %fusion.34 = f32[8,64,256,16]{2,3,1,0:T(8,128)} fusion(f32[8,64,256,16]{2,1,3,0:T(8,128)S(1)} %fusion.37, f32[256]{0:T(256)S(1)} %fusion.99, s32[256]{0:T(256)S(1)} %multiply_add_fusion.1), kind=kOutput, calls=%fused_computation.43 | convolution fusion | flops 6443433984 | bytes 16779264 | tf_op jit(solution)/shard_map/ia,cjak->cjik/dot_general | solution.py:104
  625.3 61.7 %copy.38 = f32[8,64,256,16]{0,3,2,1:T(8,128)} copy(f32[8,64,256,16]{2,3,1,0:T(8,128)} %fusion.34) | data formatting | bytes 16777216 | tf_op jit(solution)/shard_map/reshape | solution.py:110
  687.0 38.6 %scatter_custom_fusion = f32[8,8192]{0,1:T(8,128)} fusion(s32[4096]{0:T(1024)S(1)} %get-tuple-element.21, f32[]{:T(128)} %constant.42.clone.1, f32[]{:T(128)} %constant.125.clone.1, pred[4096]{0:T(1024)(128)(4,1)S(1)} %compare_and_fusion.1, pred[4096]{0:T(1024)(128)(4,1)S(1)} %compare_and_fusion, f32[8,262144]{0,1:T(8,128)} %bitcast.19, ...), kind=kCustom, calls=%fused_computation.45 | custom fusion | flops 65536 | bytes 134505984 | tf_op jit(solution)/shard_map/scatter | solution.py:112
  725.5 0.0 reduce-scatter.2.cloned.1.call-update
  725.6 49.1 %reduce-scatter.2.cloned.1.call-done = f32[8,1024]{0,1:T(8,128)} async-done(((f32[8,8192]{0,1:T(8,128)}), f32[8,1024]{0,1:T(8,128)}) %reduce-scatter.2.cloned.1.call-update) | async-done | bytes 32784 | tf_op jit(solution)/shard_map/reduce_scatter | solution.py:113
  774.7 1.8 copy.32
  (29 shorter events, 0.2 us)
Async XLA Ops:
  6.5 304.3 %copy-start = (f32[64,64]{1,0:T(8,128)S(1)}, f32[64,64]{1,0:T(8,128)}, u32[]{:S(2)}) copy-start(f32[64,64]{1,0:T(8,128)} %param.19) | copy-start | bytes 49156
  6.5 23.2 %copy-start.2 = (s32[32,64,512]{2,1,0:T(8,128)S(1)}, s32[32,64,512]{2,1,0:T(8,128)}, u32[]{:S(2)}) copy-start(s32[32,64,512]{2,1,0:T(8,128)} %param.18) | copy-start | bytes 12582916
  10.0 23.1 %collective-permute-start = (bf16[8,32,1,512]{3,1,2,0:T(8,128)(2,1)S(1)}, bf16[8,32,1,512]{3,1,2,0:T(8,128)(2,1)S(1)}, u32[]{:S(2)}, u32[]{:S(2)}) collective-permute-start(bf16[8,32,1,512]{3,1,2,0:T(8,128)(2,1)S(1)} %copy.41), channel_id=1, source_target_pairs={{0,4},{4,8},{8,12},{1,5},{5,9},{9,13},{2,6},{6,10},{10,14},{3,7},{... | collective-permute-start | bytes 786440 | tf_op jit(solution)/shard_map/ppermute | solution.py:29
  15.0 18.5 %collective-permute-start.1 = (bf16[8,32,1,512]{3,1,2,0:T(8,128)(2,1)S(1)}, bf16[8,32,1,512]{3,1,2,0:T(8,128)(2,1)S(1)}, u32[]{:S(2)}, u32[]{:S(2)}) collective-permute-start(bf16[8,32,1,512]{3,1,2,0:T(8,128)(2,1)S(1)} %copy.42), channel_id=1, source_target_pairs={{4,0},{8,4},{12,8},{5,1},{9,5},{13,9},{6,2},{10,6},{14,10},{7,3},{... | collective-permute-start | bytes 786440 | tf_op jit(solution)/shard_map/ppermute | solution.py:31
  32.3 22.9 %copy-start.8 = (f32[512]{0:T(512)}, f32[512]{0:T(512)S(1)}, u32[]{:S(2)}) copy-start(f32[512]{0:T(512)S(1)} %select_multiply_fusion) | copy-start | bytes 6148
  139.4 4.9 copy-start.1
  139.4 4.9 copy-start.5
  139.4 4.9 slice-start
  287.7 20.3 %copy-start.3 = (s32[4096]{0:T(1024)S(1)}, s32[4096]{0:T(1024)}, u32[]{:S(2)}) copy-start(s32[4096]{0:T(1024)} %param.23) | copy-start | bytes 49156
  287.7 23.7 %copy-start.4 = (s32[4096]{0:T(1024)S(1)}, s32[4096]{0:T(1024)}, u32[]{:S(2)}) copy-start(s32[4096]{0:T(1024)} %param.20) | copy-start | bytes 49156
  287.7 23.7 %copy-start.6 = (s32[4096]{0:T(1024)S(1)}, s32[4096]{0:T(1024)}, u32[]{:S(2)}) copy-start(s32[4096]{0:T(1024)} %param.21) | copy-start | bytes 49156
  287.7 23.8 %copy-start.7 = (s32[4096]{0:T(1024)S(1)}, s32[4096]{0:T(1024)}, u32[]{:S(2)}) copy-start(s32[4096]{0:T(1024)} %param.22) | copy-start | bytes 49156
  302.1 189.4 %all-to-all-start = ((f32[4,1,524288]{2,1,0:T(1,128)}), f32[4,1,524288]{2,1,0:T(1,128)}, u32[]{:S(2)}, u32[]{:S(2)}) async-start(f32[4,1,524288]{2,1,0:T(1,128)} %reshape.118), calls=%async_computation | async-start | bytes 16777216 | tf_op jit(solution)/shard_map/all_to_all | solution.py:11
  308.0 466.7 %reduce-scatter.2.cloned.1.call-start = ((), (), s32[]{:S(2)}) async-start(), calls=%async_computation.3 | async-start | bytes 4718592 | tf_op jit(solution)/shard_map/reduce_scatter | solution.py:113
Sparse Core Ops, SparseCore 0:
  725.7 48.9 reduce-scatter.1
